TPU v7x, 128 devices: a whole 4x4x4 slice. The times are simulated.
128 devices in a mesh: dom: 16 (over z, y), grp: 8 (over x, core).
Axes of the slice: x: 4, y: 4, z: 4, core: 2. Of those that a mesh axis runs over, the one named last changes fastest.
Arguments:
- residual_in: bfloat16 [1024, 32, 625], P(('dom', 'grp')), may hold values from -6 to 6
- block_inverse: bfloat16 [1024, 625, 625], P(('dom', 'grp')), may hold values from -0.25 to 0.25
- coupling: bfloat16 [2048, 625, 625], P(('dom', 'grp')), may hold values from -0.25 to 0.25
- tile_region: int32 [2048, 1], P(('dom', 'grp')), may hold values from 0 to 15; in each aligned block of 16 rows (0 to 15, 16 to 31, ...) at most 2 rows name the same one
- tile_source: int32 [2048], P(('dom', 'grp')), may hold values from 0 to 7
- tile_target: int32 [2048], P(('dom', 'grp')), may hold values from 0 to 7
- interface_basis: bfloat16 [1024, 625, 64], P(('dom', 'grp')), may hold values from -0.25 to 0.25
- reduced_inverse: float32 [16, 64, 64], P('dom'), may hold values from -0.75 to 0.75
Outputs:
- preconditioned: float32 [1024, 32, 625], P(('dom', 'grp'))
Inputs may be any that keep to these rules, and one draw needn't show every extreme that they name: `tile_region`: among the 16 tiles of one device, at most 2 name the same region; in every draw some device names some region exactly 2 times.
All inputs are finite; a program needn't handle non-finite values.
Results may differ from a plain program's by a relative error of at most 0.013.
Values may be sent and summed in bfloat16 or wider, within the bound.
No kernel may reach another device: no remote copies, remote signals or barrier semaphores. Data moves between devices by JAX's collectives and lax.ppermute only.
A program may use at most 256 MiB of HBM per device.

v0:
```python
import jax
import jax.numpy as jnp
from jax import lax
from jax.sharding import PartitionSpec as P

CAP = 2
LANE = 128


def group_sum(value, axis):
    size = lax.axis_size(axis)
    if size & size - 1:
        return lax.psum(value, axis)
    bit = 1
    while bit < size:
        pairs = [(i, i ^ bit) for i in range(size)]
        value = value + lax.ppermute(value, axis, pairs)
        bit *= 2
    return value


def shards(
    residual_in,
    block_inverse,
    coupling,
    tile_region,
    tile_source,
    tile_target,
    interface_basis,
    reduced_inverse,
):
    regions = lax.axis_size("dom")
    slots = regions * CAP
    elements = residual_in.shape[0]
    vectors = residual_in.shape[1]
    width = residual_in.shape[2]
    tiles = coupling.shape[0]
    padded = -(-(width + 1) // LANE) * LANE
    initial = jnp.einsum(
        "ekb,ebc->ekc", residual_in, block_inverse, preferred_element_type=jnp.float32
    ).astype(jnp.bfloat16)
    info = lax.optimization_barrier(jnp.concatenate([tile_region[:, 0], tile_source, tile_target]))
    destination = info[:tiles]
    tile_source = info[tiles : 2 * tiles]
    tile_target = info[2 * tiles :]
    order = jnp.arange(tiles, dtype=jnp.int32)
    same = destination[:, None] == destination[None, :]
    tile_rank = jnp.sum(same & (order[None, :] < order[:, None]), axis=1).astype(jnp.int32)
    slot_index = destination * CAP + tile_rank
    slot_ids = jnp.arange(slots, dtype=jnp.int32)
    hit = slot_index[None, :] == slot_ids[:, None]
    slot_tile = jnp.where(
        jnp.any(hit, axis=1), jnp.sum(jnp.where(hit, order[None, :], 0), axis=1), tiles
    ).astype(jnp.int32)
    sources = initial[tile_source]
    middle = tiles // 2
    local_products = jnp.concatenate(
        [
            jnp.einsum(
                "tkb,tbc->tkc",
                sources[:middle],
                coupling[:middle],
                preferred_element_type=jnp.float32,
            ),
            jnp.einsum(
                "tkb,tbc->tkc",
                sources[middle:],
                coupling[middle:],
                preferred_element_type=jnp.float32,
            ),
        ],
        axis=0,
    ).astype(jnp.bfloat16)
    marks = jnp.concatenate([tile_target, jnp.full((1,), -1, jnp.int32)]).astype(jnp.bfloat16)
    column = lax.broadcasted_iota(jnp.int32, (tiles + 1, vectors, padded - width), 2)
    row = lax.broadcasted_iota(jnp.int32, (tiles + 1, vectors, padded - width), 1)
    tail = jnp.where((column == 0) & (row == 0), marks[:, None, None], jnp.bfloat16(0))
    body = jnp.concatenate([local_products, jnp.zeros((1, vectors, width), jnp.bfloat16)], axis=0)
    extended = jnp.concatenate([body, tail], axis=2)
    product_buffer = extended[slot_tile]
    received = lax.all_to_all(
        product_buffer.reshape(regions, CAP, vectors, padded),
        "dom",
        split_axis=0,
        concat_axis=0,
        tiled=True,
    ).reshape(slots, vectors, padded)
    targets = received[:, 0, width].astype(jnp.int32)
    products = received[:, :, :width]
    selector = (targets[None, :] == jnp.arange(elements, dtype=jnp.int32)[:, None]).astype(
        jnp.bfloat16
    )
    coupled = jnp.einsum("es,skc->ekc", selector, products, preferred_element_type=jnp.float32)
    corrected_in = (residual_in.astype(jnp.float32) - coupled).astype(jnp.bfloat16)
    projected = jnp.einsum(
        "ebc,ecm->ebm", block_inverse, interface_basis, preferred_element_type=jnp.float32
    )
    partial_reduced = jnp.einsum(
        "ekb,ebm->km",
        corrected_in,
        lax.optimization_barrier(projected.astype(jnp.bfloat16)),
        preferred_element_type=jnp.float32,
    )
    reduced = group_sum(partial_reduced, "grp")
    half = elements // 2
    second = jnp.concatenate(
        [
            jnp.einsum(
                "ekb,ebc->ekc",
                corrected_in[:half],
                block_inverse[:half],
                preferred_element_type=jnp.float32,
            ),
            jnp.einsum(
                "ekb,ebc->ekc",
                corrected_in[half:],
                block_inverse[half:],
                preferred_element_type=jnp.float32,
            ),
        ],
        axis=0,
    )
    solved = jnp.dot(
        reduced,
        reduced_inverse[0],
        precision=lax.Precision.HIGHEST,
        preferred_element_type=jnp.float32,
    ).astype(jnp.bfloat16)
    correction = jnp.einsum(
        "km,ebm->ekb", solved, interface_basis, preferred_element_type=jnp.float32
    )
    return second + correction


def solution(mesh):
    return jax.shard_map(
        shards,
        mesh=mesh,
        in_specs=(
            P(("dom", "grp"), None, None),
            P(("dom", "grp"), None, None),
            P(("dom", "grp"), None, None),
            P(("dom", "grp"), None),
            P(("dom", "grp")),
            P(("dom", "grp")),
            P(("dom", "grp"), None, None),
            P("dom", None, None),
        ),
        out_specs=P(("dom", "grp"), None, None),
        check_vma=False,
    )
```

profile of v0, /device:TPU:0, one launch (start us, length us, event | category | flops | bytes accessed | tf_op | source)
XLA Modules:
  0.0 69.1 jit_solution(7914102216442023581)
XLA Ops:
  0.0 0.0 copy-start
  0.0 0.8 %pad_add_fusion = s32[48]{0:T(128)S(1)} fusion(s32[16]{0:T(128)} %param.13, s32[16]{0:T(128)} %param.12, s32[16]{0:T(128)} %bitcast.36), kind=kLoop, calls=%fused_computation.49 | loop fusion | flops 96 | bytes 384 | tf_op jit(solution)/shard_map/concatenate | solution.py:42
  0.8 0.2 convert_reduce_fusion.1
  1.0 0.1 multiply_add_fusion
  1.1 0.1 fusion.32
  1.2 0.1 select_reduce_fusion
  1.3 0.0 copy-start.2
  1.3 0.0 copy-start.4
  1.3 11.4 %fusion.40 = (bf16[8,625,625]{2,0,1:T(8,128)(2,1)}, bf16[8,625,625]{2,0,1:T(8,128)(2,1)}) fusion(bf16[16,625,625]{2,0,1:T(8,128)(2,1)} %param.10), kind=kLoop, calls=%fused_computation.56 | loop fusion | bytes 25000000 | tf_op jit(solution)/shard_map/slice | solution.py:62
  12.7 0.0 copy-done.2
  12.7 0.0 copy-done.4
  12.7 2.3 %convolution_convert_fusion.1 = bf16[8,32,625]{2,1,0:T(8,128)(2,1)S(1)} fusion(bf16[8,32,625]{2,1,0:T(8,128)(2,1)S(1)} %copy-done.4, bf16[8,625,625]{2,0,1:T(8,128)(2,1)S(1)} %copy-done.2), kind=kOutput, calls=%fused_computation.22 | convolution fusion | flops 200160000 | bytes 6890000 | tf_op jit(solution)/shard_map/ekb,ebc->ekc/dot_general | solution.py:39
  15.0 0.0 slice-start.2
  15.0 1.5 %gather_fusion = bf16[16,32,625]{2,1,0:T(8,128)(2,1)} fusion(bf16[8,32,625]{2,1,0:T(8,128)(2,1)S(1)} %convolution_convert_fusion.1, s32[1024]{0:T(1024)S(1)} %pad_clamp_fusion.1), kind=kCustom, calls=%fused_computation | custom fusion | bytes 1280064 | tf_op jit(solution)/shard_map/gather | solution.py:55
  16.4 0.0 slice-start.3
  16.4 0.0 copy-start.3
  16.4 4.3 %fusion.19 = bf16[8,32,625]{2,1,0:T(8,128)(2,1)S(1)} fusion(bf16[16,32,625]{2,1,0:T(8,128)(2,1)} %gather_fusion, bf16[8,625,625]{2,0,1:T(8,128)(2,1)} %get-tuple-element.5), kind=kOutput, calls=%fused_computation.20 | convolution fusion | flops 200160000 | bytes 7210000 | tf_op jit(solution)/shard_map/tkb,tbc->tkc/dot_general | solution.py:59
  20.7 0.0 slice-done.2
  20.7 0.1 slice-done.3
  20.8 0.0 copy-done.3
  20.8 1.2 %fusion.22 = bf16[8,32,625]{2,1,0:T(8,128)(2,1)S(1)} fusion(bf16[16,32,625]{2,1,0:T(8,128)(2,1)S(1)} %copy-done.3, bf16[8,625,625]{2,0,1:T(8,128)(2,1)S(1)} %bitcast.33), kind=kOutput, calls=%fused_computation.21 | convolution fusion | flops 200160000 | bytes 7210000 | tf_op jit(solution)/shard_map/tkb,tbc->tkc/dot_general | solution.py:65
  22.0 0.1 slice.45
  22.1 0.1 fusion.26
  22.1 0.1 pad_maximum_fusion.1
  22.2 0.1 and_select_fusion
  22.3 0.1 pad_maximum_fusion
  22.4 1.9 %gather_fusion.1 = bf16[32,32,640]{2,1,0:T(8,128)(2,1)} fusion(bf16[17,32,640]{2,1,0:T(8,128)(2,1)S(1)} %pad_maximum_fusion, s32[1024]{0:T(1024)S(1)} %pad_clamp_fusion), kind=kCustom, calls=%fused_computation.1 | custom fusion | bytes 2621568 | tf_op jit(solution)/shard_map/gather | solution.py:80
  24.3 0.0 slice-start
  24.3 8.3 %all-to-all-start = ((bf16[16,2,32,640]{3,2,1,0:T(8,128)(2,1)}), bf16[16,2,32,640]{3,2,1,0:T(8,128)(2,1)}, u32[]{:S(2)}, u32[]{:S(2)}) async-start(bf16[16,2,32,640]{3,2,1,0:T(8,128)(2,1)} %bitcast.34), calls=%async_computation | async-start | bytes 2621440 | tf_op jit(solution)/shard_map/all_to_all | solution.py:81
  32.6 0.0 slice-start.1
  32.7 6.5 %copy.30 = bf16[8,625,625]{2,1,0:T(8,128)(2,1)} copy(bf16[8,625,625]{2,0,1:T(8,128)(2,1)} %param.9) | data formatting | bytes 12500000 | tf_op args[1]
  39.2 0.0 copy-done
  39.2 0.0 slice-done
  39.2 0.0 slice-done.1
  39.2 2.2 %convolution_convert_fusion = bf16[8,625,64]{1,2,0:T(8,128)(2,1)S(1)} fusion(bf16[8,625,64]{1,2,0:T(8,128)(2,1)S(1)} %copy-done, bf16[8,625,625]{2,0,1:T(8,128)(2,1)S(1)} %bitcast.31), kind=kOutput, calls=%fused_computation.13 | convolution fusion | flops 400320000 | bytes 7530000 | tf_op jit(solution)/shard_map/ebc,ecm->ebm/dot_general | solution.py:95
  41.4 0.0 copy-start.5
  41.4 12.2 %all-to-all-done = bf16[16,2,32,640]{3,2,1,0:T(8,128)(2,1)} async-done(((bf16[16,2,32,640]{3,2,1,0:T(8,128)(2,1)}), bf16[16,2,32,640]{3,2,1,0:T(8,128)(2,1)}, u32[]{:S(2)}, u32[]{:S(2)}) %all-to-all-start) | async-done | bytes 1310752 | tf_op jit(solution)/shard_map/all_to_all | solution.py:81
  53.6 0.0 copy-start.1
  53.6 1.1 %slice.57 = bf16[32,1,1]{2,1,0:T(2,128)(2,1)S(1)} slice(bf16[32,32,640]{2,1,0:T(8,128)(2,1)} %bitcast.4), slice={[0:32], [0:1], [625:626]} | slice | bytes 128 | tf_op jit(solution)/shard_map/slice | solution.py:88
  54.7 0.1 convert_reduce_fusion
  54.8 2.2 %fusion.16 = bf16[8,32,625]{2,0,1:T(8,128)(2,1)S(1)} fusion(bf16[32,32,625]{2,1,0:T(8,128)(2,1)} %bitcast.29, bf16[8,32,625]{2,1,0:T(8,128)(2,1)} %param.8, s32[32]{0:T(128)S(1)} %convert_reduce_fusion), kind=kOutput, calls=%fused_computation.19 | convolution fusion | flops 10720256 | bytes 1920128 | tf_op jit(solution)/shard_map/es,skc->ekc/dot_general | solution.py:93
  57.0 0.3 convolution_bitcast_fusion.1
  57.3 0.0 collective-permute-start
  57.3 0.1 fusion.41
  57.4 1.1 %collective-permute-done = f32[32,64]{1,0:T(8,128)S(1)} collective-permute-done((f32[32,64]{1,0:T(8,128)S(1)}, f32[32,64]{1,0:T(8,128)S(1)}, u32[]{:S(2)}, u32[]{:S(2)}) %collective-permute-start) | collective-permute-done | bytes 8224 | tf_op jit(solution)/shard_map/ppermute | solution.py:17
  58.5 1.5 %collective-permute-start.1 = (f32[32,64]{1,0:T(8,128)S(1)}, f32[32,64]{1,0:T(8,128)S(1)}, u32[]{:S(2)}, u32[]{:S(2)}) collective-permute-start(f32[32,64]{1,0:T(8,128)S(1)} %add.37), channel_id=1, source_target_pairs={{0,2},{1,3},{2,0},{3,1},{4,6},{5,7},{6,4},{7,5},{8,10},{9,11},{10,... | collective-permute-start | bytes 24584 | tf_op jit(solution)/shard_map/ppermute | solution.py:17
  60.0 2.5 %fusion.4 = f32[4,32,625]{2,1,0:T(8,128)S(1)} fusion(bf16[8,625,625]{2,1,0:T(8,128)(2,1)} %copy.30, bf16[4,32,625]{2,0,1:T(4,128)(2,1)S(1)} %get-tuple-element.8), kind=kOutput, calls=%fused_computation.6 | convolution fusion | flops 100000000 | bytes 3715840 | tf_op jit(solution)/shard_map/ekb,ebc->ekc/dot_general | solution.py:114
  62.5 0.0 collective-permute-done.1
  62.5 2.8 %collective-permute-start.2 = (f32[32,64]{1,0:T(8,128)S(1)}, f32[32,64]{1,0:T(8,128)S(1)}, u32[]{:S(2)}, u32[]{:S(2)}) collective-permute-start(f32[32,64]{1,0:T(8,128)S(1)} %add.38), channel_id=1, source_target_pairs={{0,4},{1,5},{2,6},{3,7},{4,0},{5,1},{6,2},{7,3},{8,12},{9,13},{10,... | collective-permute-start | bytes 24584 | tf_op jit(solution)/shard_map/ppermute | solution.py:17
  65.3 0.0 copy-done.1
  65.3 0.6 fusion.6
  66.0 1.9 %collective-permute-done.2 = f32[32,64]{1,0:T(8,128)S(1)} collective-permute-done((f32[32,64]{1,0:T(8,128)S(1)}, f32[32,64]{1,0:T(8,128)S(1)}, u32[]{:S(2)}, u32[]{:S(2)}) %collective-permute-start.2) | collective-permute-done | bytes 8224 | tf_op jit(solution)/shard_map/ppermute | solution.py:17
  67.8 0.0 copy-done.5
  67.8 0.1 fusion.25
  68.0 1.1 %fusion.15 = f32[8,32,625]{2,1,0:T(8,128)} fusion(bf16[32,64,1]{1,0,2:T(8,128)(2,1)S(1)} %fusion.25, bf16[8,625,64]{1,2,0:T(8,128)(2,1)S(1)} %copy-done, f32[4,32,625]{2,1,0:T(8,128)S(1)} %fusion.4, f32[4,32,625]{2,1,0:T(8,128)S(1)} %fusion.6), kind=kOutput, calls=%fused_computation.18 | convolution fusion | flops 20800000 | bytes 1924096 | tf_op jit(solution)/shard_map/km,ebm->ekb/dot_general | solution.py:129
  (10 shorter events, 0.0 us)
Async XLA Ops:
  0.0 39.2 %copy-start = (bf16[8,625,64]{1,2,0:T(8,128)(2,1)S(1)}, bf16[8,625,64]{1,2,0:T(8,128)(2,1)}, u32[]{:S(2)}) copy-start(bf16[8,625,64]{1,2,0:T(8,128)(2,1)} %param.14) | copy-start | bytes 1920004
  1.3 11.4 %copy-start.2 = (bf16[8,625,625]{2,0,1:T(8,128)(2,1)S(1)}, bf16[8,625,625]{2,0,1:T(8,128)(2,1)}, u32[]{:S(2)}) copy-start(bf16[8,625,625]{2,0,1:T(8,128)(2,1)} %param.9) | copy-start | bytes 18750004
  1.3 11.4 %copy-start.4 = (bf16[8,32,625]{2,1,0:T(8,128)(2,1)S(1)}, bf16[8,32,625]{2,1,0:T(8,128)(2,1)}, u32[]{:S(2)}) copy-start(bf16[8,32,625]{2,1,0:T(8,128)(2,1)} %param.8) | copy-start | bytes 960004
  15.0 5.7 %slice-start.2 = ((s8[6400000]{0:T(1024)(128)(4,1)}), s8[2205696]{0:T(1024)(128)(4,1)S(1)}, s32[]{:S(2)}) async-start(s8[6400000]{0:T(1024)(128)(4,1)} %bitcast.32), calls=%async_computation.3 | async-start | bytes 4411392
  16.4 4.4 %slice-start.3 = ((s8[6400000]{0:T(1024)(128)(4,1)}), s8[4194304]{0:T(1024)(128)(4,1)S(1)}, s32[]{:S(2)}) async-start(s8[6400000]{0:T(1024)(128)(4,1)} %bitcast.32), calls=%async_computation.4 | async-start | bytes 8388608
  16.4 4.4 %copy-start.3 = (bf16[16,32,625]{2,1,0:T(8,128)(2,1)S(1)}, bf16[16,32,625]{2,1,0:T(8,128)(2,1)}, u32[]{:S(2)}) copy-start(bf16[16,32,625]{2,1,0:T(8,128)(2,1)} %gather_fusion) | copy-start | bytes 1920004
  24.3 14.9 %slice-start = ((s8[6400000]{0:T(1024)(128)(4,1)}), s8[2205696]{0:T(1024)(128)(4,1)S(1)}, s32[]{:S(2)}) async-start(s8[6400000]{0:T(1024)(128)(4,1)} %bitcast.30), calls=%async_computation.1 | async-start | bytes 4411392
  24.3 29.3 %all-to-all-start = ((bf16[16,2,32,640]{3,2,1,0:T(8,128)(2,1)}), bf16[16,2,32,640]{3,2,1,0:T(8,128)(2,1)}, u32[]{:S(2)}, u32[]{:S(2)}) async-start(bf16[16,2,32,640]{3,2,1,0:T(8,128)(2,1)} %bitcast.34), calls=%async_computation | async-start | bytes 2621440 | tf_op jit(solution)/shard_map/all_to_all | solution.py:81
  32.6 6.5 %slice-start.1 = ((s8[6400000]{0:T(1024)(128)(4,1)}), s8[4194304]{0:T(1024)(128)(4,1)S(1)}, s32[]{:S(2)}) async-start(s8[6400000]{0:T(1024)(128)(4,1)} %bitcast.30), calls=%async_computation.2 | async-start | bytes 8388608
  41.4 26.4 %copy-start.5 = (f32[1,64,64]{2,1,0:T(8,128)S(1)}, f32[1,64,64]{2,1,0:T(8,128)}, u32[]{:S(2)}) copy-start(f32[1,64,64]{2,1,0:T(8,128)} %param.15) | copy-start | bytes 49156
  53.6 11.7 %copy-start.1 = (bf16[8,625,625]{2,1,0:T(8,128)(2,1)S(1)}, bf16[8,625,625]{2,1,0:T(8,128)(2,1)}, u32[]{:S(2)}) copy-start(bf16[8,625,625]{2,1,0:T(8,128)(2,1)} %copy.30) | copy-start | bytes 18750004
  57.3 1.2 %collective-permute-start = (f32[32,64]{1,0:T(8,128)S(1)}, f32[32,64]{1,0:T(8,128)S(1)}, u32[]{:S(2)}, u32[]{:S(2)}) collective-permute-start(f32[32,64]{1,0:T(8,128)S(1)} %convolution_bitcast_fusion.1), channel_id=1, source_target_pairs={{0,1},{1,0},{2,3},{3,2},{4,5},{5,4},{6,7},{7,6},{8,9},{9,8},{10,11... | collective-permute-start | bytes 24584 | tf_op jit(solution)/shard_map/ppermute | solution.py:17
  58.5 4.0 %collective-permute-start.1 = (f32[32,64]{1,0:T(8,128)S(1)}, f32[32,64]{1,0:T(8,128)S(1)}, u32[]{:S(2)}, u32[]{:S(2)}) collective-permute-start(f32[32,64]{1,0:T(8,128)S(1)} %add.37), channel_id=1, source_target_pairs={{0,2},{1,3},{2,0},{3,1},{4,6},{5,7},{6,4},{7,5},{8,10},{9,11},{10,... | collective-permute-start | bytes 24584 | tf_op jit(solution)/shard_map/ppermute | solution.py:17
  62.5 5.3 %collective-permute-start.2 = (f32[32,64]{1,0:T(8,128)S(1)}, f32[32,64]{1,0:T(8,128)S(1)}, u32[]{:S(2)}, u32[]{:S(2)}) collective-permute-start(f32[32,64]{1,0:T(8,128)S(1)} %add.38), channel_id=1, source_target_pairs={{0,4},{1,5},{2,6},{3,7},{4,0},{5,1},{6,2},{7,3},{8,12},{9,13},{10,... | collective-permute-start | bytes 24584 | tf_op jit(solution)/shard_map/ppermute | solution.py:17
where the time goes:
time: 69.3 us; the launch traced here: 69.1 us
  local copies, waits for them, and re-layouts  22.6 us (33%)
  matrix products  16.7 us (24%)
  waiting for transfers between devices  15.2 us (22%)
  starting transfers between devices  12.7 us (18%)
  other arithmetic  1.77 us (3%)
    all_to_all x1, waiting for transfers between devices, shards(): lax.all_to_all(product_buffer.reshape(regions, CAP, vectors, padded), 'do...  12.2 us
    slice x1, local copies, waits for them, and re-layouts, shards(): coupling[:middle]  11.4 us
    all_to_all x1, starting transfers between devices, shards(): lax.all_to_all(product_buffer.reshape(regions, CAP, vectors, padded), 'do...  8.34 us
    unnamed x21, local copies, waits for them, and re-layouts  6.64 us
    ppermute x3, starting transfers between devices, group_sum(): value = value + lax.ppermute(value, axis, pairs)  4.31 us
    dot_general x1, matrix products, shards(): jnp.einsum('tkb,tbc->tkc', sources[:middle], coupling[:middle], preferred...  4.25 us
    ppermute x3, waiting for transfers between devices, group_sum(): value = value + lax.ppermute(value, axis, pairs)  2.94 us
    dot_general x1, matrix products, shards(): jnp.einsum('ekb,ebc->ekc', corrected_in[half:], block_inverse[half:], pre...  2.53 us
  transfers between devices with their start and end apart: 4, of which 3 were waited for; matrix products, arithmetic and copies ran while one was open for 17% of the time, Pallas kernels for 0%

commit v1 on v0

--- a/solution.py
+++ b/solution.py
@@ -5,6 +5,22 @@
 
 CAP = 2
 LANE = 128
+
+
+def pairwise_exchange(x, axis, split, join):
+    ways, here = (lax.axis_size(axis), lax.axis_index(axis))
+    width = x.shape[split] // ways
+    shape = list(x.shape)
+    shape[split] = width
+    height = shape[join]
+    shape[join] = height * ways
+    full = jnp.zeros(shape, x.dtype)
+    for mask in range(ways):
+        part = lax.dynamic_slice_in_dim(x, (here ^ mask) * width, width, axis=split)
+        if mask:
+            part = lax.ppermute(part, axis, [(d, d ^ mask) for d in range(ways)])
+        full = lax.dynamic_update_slice_in_dim(full, part, (here ^ mask) * height, axis=join)
+    return full
 
 
 def group_sum(value, axis):
@@ -78,12 +94,8 @@
     body = jnp.concatenate([local_products, jnp.zeros((1, vectors, width), jnp.bfloat16)], axis=0)
     extended = jnp.concatenate([body, tail], axis=2)
     product_buffer = extended[slot_tile]
-    received = lax.all_to_all(
-        product_buffer.reshape(regions, CAP, vectors, padded),
-        "dom",
-        split_axis=0,
-        concat_axis=0,
-        tiled=True,
+    received = pairwise_exchange(
+        product_buffer.reshape(regions, CAP, vectors, padded), "dom", 0, 0
     ).reshape(slots, vectors, padded)
     targets = received[:, 0, width].astype(jnp.int32)
     products = received[:, :, :width]

time: 69.3 us -> 90.4 us (1.30)
  starting transfers between devices: 12.7 us -> 37.6 us
  waiting for transfers between devices: 15.2 us -> 10.3 us
  matrix products: 16.7 us -> 19.8 us
  local copies, waits for them, and re-layouts: 22.6 us -> 20.1 us
    ppermute x0 -> x15, starting transfers between devices: none -> 33.3 us  [pairwise_exchange(): part = lax.ppermute(part, axis, [(d, d ^ mask) for d in range(ways)])]
    all_to_all x1 -> x0, waiting for transfers between devices: 12.2 us -> none  [shards(): lax.all_to_all(product_buffer.reshape(regions, CAP, vectors, padded), 'do...]
    all_to_all x1 -> x0, starting transfers between devices: 8.34 us -> none  [shards(): lax.all_to_all(product_buffer.reshape(regions, CAP, vectors, padded), 'do...]
    ppermute x0 -> x15, waiting for transfers between devices: none -> 7.32 us  [pairwise_exchange(): part = lax.ppermute(part, axis, [(d, d ^ mask) for d in range(ways)])]
    dot_general x1, matrix products: 2.22 us -> 6.06 us  [shards(): jnp.einsum('ebc,ecm->ebm', block_inverse, interface_basis, preferred_elem...]
    unnamed x21 -> x23, local copies, waits for them, and re-layouts: 6.64 us -> 3.64 us
    dynamic_update_slice x0 -> x16, local copies, waits for them, and re-layouts: none -> 1.24 us  [pairwise_exchange(): lax.dynamic_update_slice_in_dim(full, part, (here ^ mask) * height, axis=...]
    gather x1, local copies, waits for them, and re-layouts: 1.85 us -> 0.78 us  [shards(): product_buffer = extended[slot_tile]]
  transfers between devices with their start and end apart: 4 -> 18, of which waited for: 3 -> 4; matrix products, arithmetic and copies ran while one was open for 17% -> 16% of each run, Pallas kernels for 0% -> 0%
where the time goes in v1:
time: 90.4 us; the launch traced here: 90.2 us
  starting transfers between devices  37.6 us (42%)
  local copies, waits for them, and re-layouts  20.1 us (22%)
  matrix products  19.8 us (22%)
  waiting for transfers between devices  10.3 us (11%)
  other arithmetic  1.84 us (2%)
    ppermute x15, starting transfers between devices, pairwise_exchange(): part = lax.ppermute(part, axis, [(d, d ^ mask) for d in range(ways)])  33.3 us
    slice x1, local copies, waits for them, and re-layouts, shards(): coupling[:middle]  11.4 us
    ppermute x15, waiting for transfers between devices, pairwise_exchange(): part = lax.ppermute(part, axis, [(d, d ^ mask) for d in range(ways)])  7.32 us
    dot_general x1, matrix products, shards(): jnp.einsum('ebc,ecm->ebm', block_inverse, interface_basis, preferred_elem...  6.06 us
    ppermute x3, starting transfers between devices, group_sum(): value = value + lax.ppermute(value, axis, pairs)  4.3 us
    dot_general x1, matrix products, shards(): jnp.einsum('tkb,tbc->tkc', sources[:middle], coupling[:middle], preferred...  4.26 us
    unnamed x23, local copies, waits for them, and re-layouts  3.64 us
    ppermute x3, waiting for transfers between devices, group_sum(): value = value + lax.ppermute(value, axis, pairs)  2.96 us
  transfers between devices with their start and end apart: 18, of which 4 were waited for; matrix products, arithmetic and copies ran while one was open for 16% of the time, Pallas kernels for 0%

profile of v1, /device:TPU:0, one launch (start us, length us, event | category | flops | bytes accessed | tf_op | source)
XLA Modules:
  0.0 90.2 jit_solution(8882299802838040129)
XLA Ops:
  0.0 0.8 pad_add_fusion
  0.8 0.2 convert_reduce_fusion.1
  1.0 0.1 multiply_add_fusion
  1.1 0.1 fusion.32
  1.2 0.1 select_reduce_fusion
  1.3 11.4 %fusion.40 = (bf16[8,625,625]{2,0,1:T(8,128)(2,1)}, bf16[8,625,625]{2,0,1:T(8,128)(2,1)}) fusion(bf16[16,625,625]{2,0,1:T(8,128)(2,1)} %param.10), kind=kLoop, calls=%fused_computation.88 | loop fusion | bytes 25000000 | tf_op jit(solution)/shard_map/slice | solution.py:78
  12.7 2.3 %convolution_convert_fusion.1 = bf16[8,32,625]{2,1,0:T(8,128)(2,1)S(1)} fusion(bf16[8,32,625]{2,1,0:T(8,128)(2,1)S(1)} %copy-done.5, bf16[8,625,625]{2,0,1:T(8,128)(2,1)S(1)} %copy-done.2), kind=kOutput, calls=%fused_computation.22 | convolution fusion | flops 200160000 | bytes 6890000 | tf_op jit(solution)/shard_map/ekb,ebc->ekc/dot_general | solution.py:55
  15.0 1.5 %gather_fusion = bf16[16,32,625]{2,1,0:T(8,128)(2,1)} fusion(bf16[8,32,625]{2,1,0:T(8,128)(2,1)S(1)} %convolution_convert_fusion.1, s32[1024]{0:T(1024)S(1)} %pad_clamp_fusion.1), kind=kCustom, calls=%fused_computation | custom fusion | bytes 1280064 | tf_op jit(solution)/shard_map/gather | solution.py:71
  16.5 4.3 %fusion.19 = bf16[8,32,625]{2,1,0:T(8,128)(2,1)S(1)} fusion(bf16[16,32,625]{2,1,0:T(8,128)(2,1)} %gather_fusion, bf16[8,625,625]{2,0,1:T(8,128)(2,1)} %get-tuple-element.5), kind=kOutput, calls=%fused_computation.20 | convolution fusion | flops 200160000 | bytes 7210000 | tf_op jit(solution)/shard_map/tkb,tbc->tkc/dot_general | solution.py:75
  20.7 0.1 slice-done.3
  20.8 1.2 %fusion.22 = bf16[8,32,625]{2,1,0:T(8,128)(2,1)S(1)} fusion(bf16[16,32,625]{2,1,0:T(8,128)(2,1)S(1)} %copy-done.3, bf16[8,625,625]{2,0,1:T(8,128)(2,1)S(1)} %bitcast.33), kind=kOutput, calls=%fused_computation.21 | convolution fusion | flops 200160000 | bytes 7210000 | tf_op jit(solution)/shard_map/tkb,tbc->tkc/dot_general | solution.py:81
  22.2 0.1 pad_maximum_fusion.1
  22.3 0.1 and_select_fusion
  22.4 0.1 pad_maximum_fusion
  22.5 0.8 gather_fusion.1
  23.3 0.2 constant_dynamic-slice_fusion
  23.6 1.8 %collective-permute-start = (bf16[1,2,32,640]{3,2,1,0:T(8,128)(2,1)S(1)}, bf16[1,2,32,640]{3,2,1,0:T(8,128)(2,1)S(1)}, u32[]{:S(2)}, u32[]{:S(2)}) collective-permute-start(bf16[1,2,32,640]{3,2,1,0:T(8,128)(2,1)S(1)} %get-tuple-element.21), channel_id=1, source_target_pairs={{0,8},{8,0},{16,24},{24,16},{32,40},{40,32},{48,56},{56,48},{64,72... | collective-permute-start | bytes 245768 | tf_op jit(solution)/shard_map/ppermute | solution.py:21
  25.3 2.9 %collective-permute-start.1 = (bf16[1,2,32,640]{3,2,1,0:T(8,128)(2,1)S(1)}, bf16[1,2,32,640]{3,2,1,0:T(8,128)(2,1)S(1)}, u32[]{:S(2)}, u32[]{:S(2)}) collective-permute-start(bf16[1,2,32,640]{3,2,1,0:T(8,128)(2,1)S(1)} %get-tuple-element.20), channel_id=1, source_target_pairs={{0,16},{8,24},{16,0},{24,8},{32,48},{40,56},{48,32},{56,40},{64,80... | collective-permute-start | bytes 245768 | tf_op jit(solution)/shard_map/ppermute | solution.py:21
  28.2 0.1 collective-permute-start.2
  28.3 2.0 %collective-permute-start.3 = (bf16[1,2,32,640]{3,2,1,0:T(8,128)(2,1)S(1)}, bf16[1,2,32,640]{3,2,1,0:T(8,128)(2,1)S(1)}, u32[]{:S(2)}, u32[]{:S(2)}) collective-permute-start(bf16[1,2,32,640]{3,2,1,0:T(8,128)(2,1)S(1)} %get-tuple-element.18), channel_id=1, source_target_pairs={{0,32},{8,40},{16,48},{24,56},{32,0},{40,8},{48,16},{56,24},{64,96... | collective-permute-start | bytes 245768 | tf_op jit(solution)/shard_map/ppermute | solution.py:21
  30.4 6.1 %convolution_convert_fusion = bf16[8,625,64]{1,2,0:T(8,128)(2,1)} fusion(bf16[8,625,64]{1,2,0:T(8,128)(2,1)S(1)} %copy-done, bf16[8,625,625]{2,0,1:T(8,128)(2,1)} %param.9), kind=kOutput, calls=%fused_computation.13 | convolution fusion | flops 400320000 | bytes 7530000 | tf_op jit(solution)/shard_map/ebc,ecm->ebm/dot_general | solution.py:107
  36.4 0.7 broadcast_in_dim.46
  37.1 0.1 copy_dynamic-update-slice_fusion.15
  37.2 3.5 %copy.60 = bf16[8,625,625]{2,1,0:T(8,128)(2,1)} copy(bf16[8,625,625]{2,0,1:T(8,128)(2,1)S(1)} %bitcast.31) | data formatting | bytes 12500000 | tf_op args[1]
  40.8 5.2 %collective-permute-start.5 = (bf16[1,2,32,640]{3,2,1,0:T(8,128)(2,1)S(1)}, bf16[1,2,32,640]{3,2,1,0:T(8,128)(2,1)S(1)}, u32[]{:S(2)}, u32[]{:S(2)}) collective-permute-start(bf16[1,2,32,640]{3,2,1,0:T(8,128)(2,1)S(1)} %get-tuple-element.16), channel_id=1, source_target_pairs={{0,48},{8,56},{16,32},{24,40},{32,16},{40,24},{48,0},{56,8},{64,11... | collective-permute-start | bytes 245768 | tf_op jit(solution)/shard_map/ppermute | solution.py:21
  45.9 0.1 copy_dynamic-update-slice_fusion.14
  46.0 0.3 collective-permute-start.6
  46.3 0.1 copy_dynamic-update-slice_fusion.13
  46.4 3.9 %collective-permute-start.7 = (bf16[1,2,32,640]{3,2,1,0:T(8,128)(2,1)S(1)}, bf16[1,2,32,640]{3,2,1,0:T(8,128)(2,1)S(1)}, u32[]{:S(2)}, u32[]{:S(2)}) collective-permute-start(bf16[1,2,32,640]{3,2,1,0:T(8,128)(2,1)S(1)} %get-tuple-element.14), channel_id=1, source_target_pairs={{0,64},{8,72},{16,80},{24,88},{32,96},{40,104},{48,112},{56,120},{... | collective-permute-start | bytes 245768 | tf_op jit(solution)/shard_map/ppermute | solution.py:21
  50.3 0.1 copy_dynamic-update-slice_fusion.12
  50.4 0.3 collective-permute-start.8
  50.7 0.1 copy_dynamic-update-slice_fusion.11
  50.8 6.5 %collective-permute-start.9 = (bf16[1,2,32,640]{3,2,1,0:T(8,128)(2,1)S(1)}, bf16[1,2,32,640]{3,2,1,0:T(8,128)(2,1)S(1)}, u32[]{:S(2)}, u32[]{:S(2)}) collective-permute-start(bf16[1,2,32,640]{3,2,1,0:T(8,128)(2,1)S(1)} %get-tuple-element.12), channel_id=1, source_target_pairs={{0,80},{8,88},{16,64},{24,72},{32,112},{40,120},{48,96},{56,104},{... | collective-permute-start | bytes 245768 | tf_op jit(solution)/shard_map/ppermute | solution.py:21
  57.3 0.1 copy_dynamic-update-slice_fusion.10
  57.4 0.2 collective-permute-start.10
  57.6 0.1 copy_dynamic-update-slice_fusion.9
  57.7 3.4 %collective-permute-start.11 = (bf16[1,2,32,640]{3,2,1,0:T(8,128)(2,1)S(1)}, bf16[1,2,32,640]{3,2,1,0:T(8,128)(2,1)S(1)}, u32[]{:S(2)}, u32[]{:S(2)}) collective-permute-start(bf16[1,2,32,640]{3,2,1,0:T(8,128)(2,1)S(1)} %get-tuple-element.10), channel_id=1, source_target_pairs={{0,96},{8,104},{16,112},{24,120},{32,64},{40,72},{48,80},{56,88},{... | collective-permute-start | bytes 245768 | tf_op jit(solution)/shard_map/ppermute | solution.py:21
  61.0 0.1 copy_dynamic-update-slice_fusion.8
  61.1 0.1 collective-permute-start.12
  61.2 0.1 copy_dynamic-update-slice_fusion.7
  61.3 6.6 %collective-permute-start.13 = (bf16[1,2,32,640]{3,2,1,0:T(8,128)(2,1)S(1)}, bf16[1,2,32,640]{3,2,1,0:T(8,128)(2,1)S(1)}, u32[]{:S(2)}, u32[]{:S(2)}) collective-permute-start(bf16[1,2,32,640]{3,2,1,0:T(8,128)(2,1)S(1)} %get-tuple-element.8), channel_id=1, source_target_pairs={{0,112},{8,120},{16,96},{24,104},{32,80},{40,88},{48,64},{56,72},{... | collective-permute-start | bytes 245768 | tf_op jit(solution)/shard_map/ppermute | solution.py:21
  67.9 0.1 copy_dynamic-update-slice_fusion.6
  68.0 0.1 collective-permute-start.14
  68.1 0.1 copy_dynamic-update-slice_fusion.5
  68.2 0.1 copy_dynamic-update-slice_fusion.4
  68.3 0.1 copy_dynamic-update-slice_fusion.3
  68.4 0.1 copy_dynamic-update-slice_fusion.2
  68.5 2.7 %collective-permute-done.13 = bf16[1,2,32,640]{3,2,1,0:T(8,128)(2,1)S(1)} collective-permute-done((bf16[1,2,32,640]{3,2,1,0:T(8,128)(2,1)S(1)}, bf16[1,2,32,640]{3,2,1,0:T(8,128)(2,1)S(1)}, u32[]{:S(2)}, u32[]{:S(2)}) %collective-permute-start.13) | collective-permute-done | bytes 81952 | tf_op jit(solution)/shard_map/ppermute | solution.py:21
  71.2 0.1 copy_dynamic-update-slice_fusion.1
  71.2 4.6 %collective-permute-done.14 = bf16[1,2,32,640]{3,2,1,0:T(8,128)(2,1)S(1)} collective-permute-done((bf16[1,2,32,640]{3,2,1,0:T(8,128)(2,1)S(1)}, bf16[1,2,32,640]{3,2,1,0:T(8,128)(2,1)S(1)}, u32[]{:S(2)}, u32[]{:S(2)}) %collective-permute-start.14) | collective-permute-done | bytes 81952 | tf_op jit(solution)/shard_map/ppermute | solution.py:21
  75.9 0.1 copy_dynamic-update-slice_fusion
  75.9 0.5 reshape.53
  76.5 0.2 convert_reduce_fusion
  76.7 1.4 %fusion.16 = bf16[8,32,625]{2,0,1:T(8,128)(2,1)S(1)} fusion(bf16[32,32,640]{2,0,1:T(8,128)(2,1)S(1)} %reshape.53, bf16[8,32,625]{2,1,0:T(8,128)(2,1)} %param.8, s32[32]{0:T(128)S(1)} %convert_reduce_fusion), kind=kOutput, calls=%fused_computation.19 | convolution fusion | flops 10720256 | bytes 1950848 | tf_op jit(solution)/shard_map/es,skc->ekc/dot_general | solution.py:105
  78.1 0.3 convolution_bitcast_fusion.1
  78.4 0.1 fusion.41
  78.5 1.1 %collective-permute-done.15 = f32[32,64]{1,0:T(8,128)S(1)} collective-permute-done((f32[32,64]{1,0:T(8,128)S(1)}, f32[32,64]{1,0:T(8,128)S(1)}, u32[]{:S(2)}, u32[]{:S(2)}) %collective-permute-start.15) | collective-permute-done | bytes 8224 | tf_op jit(solution)/shard_map/ppermute | solution.py:33
  79.6 1.5 %collective-permute-start.16 = (f32[32,64]{1,0:T(8,128)S(1)}, f32[32,64]{1,0:T(8,128)S(1)}, u32[]{:S(2)}, u32[]{:S(2)}) collective-permute-start(f32[32,64]{1,0:T(8,128)S(1)} %add.117), channel_id=1, source_target_pairs={{0,2},{1,3},{2,0},{3,1},{4,6},{5,7},{6,4},{7,5},{8,10},{9,11},{10,... | collective-permute-start | bytes 24584 | tf_op jit(solution)/shard_map/ppermute | solution.py:33
  81.1 2.5 %fusion.4 = f32[4,32,625]{2,1,0:T(8,128)S(1)} fusion(bf16[8,625,625]{2,1,0:T(8,128)(2,1)} %copy.60, bf16[4,32,625]{2,0,1:T(4,128)(2,1)S(1)} %get-tuple-element.24), kind=kOutput, calls=%fused_computation.6 | convolution fusion | flops 100000000 | bytes 3715840 | tf_op jit(solution)/shard_map/ekb,ebc->ekc/dot_general | solution.py:126
  83.7 2.8 %collective-permute-start.17 = (f32[32,64]{1,0:T(8,128)S(1)}, f32[32,64]{1,0:T(8,128)S(1)}, u32[]{:S(2)}, u32[]{:S(2)}) collective-permute-start(f32[32,64]{1,0:T(8,128)S(1)} %add.118), channel_id=1, source_target_pairs={{0,4},{1,5},{2,6},{3,7},{4,0},{5,1},{6,2},{7,3},{8,12},{9,13},{10,... | collective-permute-start | bytes 24584 | tf_op jit(solution)/shard_map/ppermute | solution.py:33
  86.5 0.6 fusion.6
  87.1 1.9 %collective-permute-done.17 = f32[32,64]{1,0:T(8,128)S(1)} collective-permute-done((f32[32,64]{1,0:T(8,128)S(1)}, f32[32,64]{1,0:T(8,128)S(1)}, u32[]{:S(2)}, u32[]{:S(2)}) %collective-permute-start.17) | collective-permute-done | bytes 8224 | tf_op jit(solution)/shard_map/ppermute | solution.py:33
  89.0 0.1 fusion.25
  89.1 1.1 %fusion.15 = f32[8,32,625]{2,1,0:T(8,128)} fusion(bf16[32,64,1]{1,0,2:T(8,128)(2,1)S(1)} %fusion.25, bf16[8,625,64]{1,2,0:T(8,128)(2,1)S(1)} %copy-done, f32[4,32,625]{2,1,0:T(8,128)S(1)} %fusion.4, f32[4,32,625]{2,1,0:T(8,128)S(1)} %fusion.6), kind=kOutput, calls=%fused_computation.18 | convolution fusion | flops 20800000 | bytes 1924096 | tf_op jit(solution)/shard_map/km,ebm->ekb/dot_general | solution.py:141
  (49 shorter events, 0.3 us)
Async XLA Ops:
  0.0 30.4 %copy-start = (bf16[8,625,64]{1,2,0:T(8,128)(2,1)S(1)}, bf16[8,625,64]{1,2,0:T(8,128)(2,1)}, u32[]{:S(2)}) copy-start(bf16[8,625,64]{1,2,0:T(8,128)(2,1)} %param.14) | copy-start | bytes 1920004
  1.3 11.4 %copy-start.2 = (bf16[8,625,625]{2,0,1:T(8,128)(2,1)S(1)}, bf16[8,625,625]{2,0,1:T(8,128)(2,1)}, u32[]{:S(2)}) copy-start(bf16[8,625,625]{2,0,1:T(8,128)(2,1)} %param.9) | copy-start | bytes 18750004
  1.3 11.4 %copy-start.5 = (bf16[8,32,625]{2,1,0:T(8,128)(2,1)S(1)}, bf16[8,32,625]{2,1,0:T(8,128)(2,1)}, u32[]{:S(2)}) copy-start(bf16[8,32,625]{2,1,0:T(8,128)(2,1)} %param.8) | copy-start | bytes 960004
  15.0 5.7 %slice-start.2 = ((s8[6400000]{0:T(1024)(128)(4,1)}), s8[2205696]{0:T(1024)(128)(4,1)S(1)}, s32[]{:S(2)}) async-start(s8[6400000]{0:T(1024)(128)(4,1)} %bitcast.32), calls=%async_computation.2 | async-start | bytes 4411392
  16.5 4.4 %slice-start.3 = ((s8[6400000]{0:T(1024)(128)(4,1)}), s8[4194304]{0:T(1024)(128)(4,1)S(1)}, s32[]{:S(2)}) async-start(s8[6400000]{0:T(1024)(128)(4,1)} %bitcast.32), calls=%async_computation.3 | async-start | bytes 8388608
  16.5 4.4 %copy-start.3 = (bf16[16,32,625]{2,1,0:T(8,128)(2,1)S(1)}, bf16[16,32,625]{2,1,0:T(8,128)(2,1)}, u32[]{:S(2)}) copy-start(bf16[16,32,625]{2,1,0:T(8,128)(2,1)} %gather_fusion) | copy-start | bytes 1920004
  23.6 17.2 %collective-permute-start = (bf16[1,2,32,640]{3,2,1,0:T(8,128)(2,1)S(1)}, bf16[1,2,32,640]{3,2,1,0:T(8,128)(2,1)S(1)}, u32[]{:S(2)}, u32[]{:S(2)}) collective-permute-start(bf16[1,2,32,640]{3,2,1,0:T(8,128)(2,1)S(1)} %get-tuple-element.21), channel_id=1, source_target_pairs={{0,8},{8,0},{16,24},{24,16},{32,40},{40,32},{48,56},{56,48},{64,72... | collective-permute-start | bytes 245768 | tf_op jit(solution)/shard_map/ppermute | solution.py:21
  25.3 20.7 %collective-permute-start.1 = (bf16[1,2,32,640]{3,2,1,0:T(8,128)(2,1)S(1)}, bf16[1,2,32,640]{3,2,1,0:T(8,128)(2,1)S(1)}, u32[]{:S(2)}, u32[]{:S(2)}) collective-permute-start(bf16[1,2,32,640]{3,2,1,0:T(8,128)(2,1)S(1)} %get-tuple-element.20), channel_id=1, source_target_pairs={{0,16},{8,24},{16,0},{24,8},{32,48},{40,56},{48,32},{56,40},{64,80... | collective-permute-start | bytes 245768 | tf_op jit(solution)/shard_map/ppermute | solution.py:21
  28.2 18.2 %collective-permute-start.2 = (bf16[1,2,32,640]{3,2,1,0:T(8,128)(2,1)S(1)}, bf16[1,2,32,640]{3,2,1,0:T(8,128)(2,1)S(1)}, u32[]{:S(2)}, u32[]{:S(2)}) collective-permute-start(bf16[1,2,32,640]{3,2,1,0:T(8,128)(2,1)S(1)} %get-tuple-element.19), channel_id=1, source_target_pairs={{0,24},{8,16},{16,8},{24,0},{32,56},{40,48},{48,40},{56,32},{64,88... | collective-permute-start | bytes 245768 | tf_op jit(solution)/shard_map/ppermute | solution.py:21
  28.3 22.1 %collective-permute-start.3 = (bf16[1,2,32,640]{3,2,1,0:T(8,128)(2,1)S(1)}, bf16[1,2,32,640]{3,2,1,0:T(8,128)(2,1)S(1)}, u32[]{:S(2)}, u32[]{:S(2)}) collective-permute-start(bf16[1,2,32,640]{3,2,1,0:T(8,128)(2,1)S(1)} %get-tuple-element.18), channel_id=1, source_target_pairs={{0,32},{8,40},{16,48},{24,56},{32,0},{40,8},{48,16},{56,24},{64,96... | collective-permute-start | bytes 245768 | tf_op jit(solution)/shard_map/ppermute | solution.py:21
  30.4 6.8 %slice-start = ((s8[6400000]{0:T(1024)(128)(4,1)}), s8[4194304]{0:T(1024)(128)(4,1)S(1)}, s32[]{:S(2)}) async-start(s8[6400000]{0:T(1024)(128)(4,1)} %bitcast.30), calls=%async_computation | async-start | bytes 8388608
  30.4 6.8 %slice-start.1 = ((s8[6400000]{0:T(1024)(128)(4,1)}), s8[2205696]{0:T(1024)(128)(4,1)S(1)}, s32[]{:S(2)}) async-start(s8[6400000]{0:T(1024)(128)(4,1)} %bitcast.30), calls=%async_computation.1 | async-start | bytes 4411392
  30.4 20.4 %collective-permute-start.4 = (bf16[1,2,32,640]{3,2,1,0:T(8,128)(2,1)S(1)}, bf16[1,2,32,640]{3,2,1,0:T(8,128)(2,1)S(1)}, u32[]{:S(2)}, u32[]{:S(2)}) collective-permute-start(bf16[1,2,32,640]{3,2,1,0:T(8,128)(2,1)S(1)} %get-tuple-element.17), channel_id=1, source_target_pairs={{0,40},{8,32},{16,56},{24,48},{32,8},{40,0},{48,24},{56,16},{64,10... | collective-permute-start | bytes 245768 | tf_op jit(solution)/shard_map/ppermute | solution.py:21
  40.8 16.6 %collective-permute-start.5 = (bf16[1,2,32,640]{3,2,1,0:T(8,128)(2,1)S(1)}, bf16[1,2,32,640]{3,2,1,0:T(8,128)(2,1)S(1)}, u32[]{:S(2)}, u32[]{:S(2)}) collective-permute-start(bf16[1,2,32,640]{3,2,1,0:T(8,128)(2,1)S(1)} %get-tuple-element.16), channel_id=1, source_target_pairs={{0,48},{8,56},{16,32},{24,40},{32,16},{40,24},{48,0},{56,8},{64,11... | collective-permute-start | bytes 245768 | tf_op jit(solution)/shard_map/ppermute | solution.py:21
  46.0 11.6 %collective-permute-start.6 = (bf16[1,2,32,640]{3,2,1,0:T(8,128)(2,1)S(1)}, bf16[1,2,32,640]{3,2,1,0:T(8,128)(2,1)S(1)}, u32[]{:S(2)}, u32[]{:S(2)}) collective-permute-start(bf16[1,2,32,640]{3,2,1,0:T(8,128)(2,1)S(1)} %get-tuple-element.15), channel_id=1, source_target_pairs={{0,56},{8,48},{16,40},{24,32},{32,24},{40,16},{48,8},{56,0},{64,12... | collective-permute-start | bytes 245768 | tf_op jit(solution)/shard_map/ppermute | solution.py:21
  46.4 14.7 %collective-permute-start.7 = (bf16[1,2,32,640]{3,2,1,0:T(8,128)(2,1)S(1)}, bf16[1,2,32,640]{3,2,1,0:T(8,128)(2,1)S(1)}, u32[]{:S(2)}, u32[]{:S(2)}) collective-permute-start(bf16[1,2,32,640]{3,2,1,0:T(8,128)(2,1)S(1)} %get-tuple-element.14), channel_id=1, source_target_pairs={{0,64},{8,72},{16,80},{24,88},{32,96},{40,104},{48,112},{56,120},{... | collective-permute-start | bytes 245768 | tf_op jit(solution)/shard_map/ppermute | solution.py:21
  50.4 10.9 %collective-permute-start.8 = (bf16[1,2,32,640]{3,2,1,0:T(8,128)(2,1)S(1)}, bf16[1,2,32,640]{3,2,1,0:T(8,128)(2,1)S(1)}, u32[]{:S(2)}, u32[]{:S(2)}) collective-permute-start(bf16[1,2,32,640]{3,2,1,0:T(8,128)(2,1)S(1)} %get-tuple-element.13), channel_id=1, source_target_pairs={{0,72},{8,64},{16,88},{24,80},{32,104},{40,96},{48,120},{56,112},{... | collective-permute-start | bytes 245768 | tf_op jit(solution)/shard_map/ppermute | solution.py:21
  50.8 17.2 %collective-permute-start.9 = (bf16[1,2,32,640]{3,2,1,0:T(8,128)(2,1)S(1)}, bf16[1,2,32,640]{3,2,1,0:T(8,128)(2,1)S(1)}, u32[]{:S(2)}, u32[]{:S(2)}) collective-permute-start(bf16[1,2,32,640]{3,2,1,0:T(8,128)(2,1)S(1)} %get-tuple-element.12), channel_id=1, source_target_pairs={{0,80},{8,88},{16,64},{24,72},{32,112},{40,120},{48,96},{56,104},{... | collective-permute-start | bytes 245768 | tf_op jit(solution)/shard_map/ppermute | solution.py:21
  57.4 10.8 %collective-permute-start.10 = (bf16[1,2,32,640]{3,2,1,0:T(8,128)(2,1)S(1)}, bf16[1,2,32,640]{3,2,1,0:T(8,128)(2,1)S(1)}, u32[]{:S(2)}, u32[]{:S(2)}) collective-permute-start(bf16[1,2,32,640]{3,2,1,0:T(8,128)(2,1)S(1)} %get-tuple-element.11), channel_id=1, source_target_pairs={{0,88},{8,80},{16,72},{24,64},{32,120},{40,112},{48,104},{56,96},{... | collective-permute-start | bytes 245768 | tf_op jit(solution)/shard_map/ppermute | solution.py:21
  57.7 10.7 %collective-permute-start.11 = (bf16[1,2,32,640]{3,2,1,0:T(8,128)(2,1)S(1)}, bf16[1,2,32,640]{3,2,1,0:T(8,128)(2,1)S(1)}, u32[]{:S(2)}, u32[]{:S(2)}) collective-permute-start(bf16[1,2,32,640]{3,2,1,0:T(8,128)(2,1)S(1)} %get-tuple-element.10), channel_id=1, source_target_pairs={{0,96},{8,104},{16,112},{24,120},{32,64},{40,72},{48,80},{56,88},{... | collective-permute-start | bytes 245768 | tf_op jit(solution)/shard_map/ppermute | solution.py:21
  61.1 7.3 %collective-permute-start.12 = (bf16[1,2,32,640]{3,2,1,0:T(8,128)(2,1)S(1)}, bf16[1,2,32,640]{3,2,1,0:T(8,128)(2,1)S(1)}, u32[]{:S(2)}, u32[]{:S(2)}) collective-permute-start(bf16[1,2,32,640]{3,2,1,0:T(8,128)(2,1)S(1)} %get-tuple-element.9), channel_id=1, source_target_pairs={{0,104},{8,96},{16,120},{24,112},{32,72},{40,64},{48,88},{56,80},{... | collective-permute-start | bytes 245768 | tf_op jit(solution)/shard_map/ppermute | solution.py:21
  61.3 9.9 %collective-permute-start.13 = (bf16[1,2,32,640]{3,2,1,0:T(8,128)(2,1)S(1)}, bf16[1,2,32,640]{3,2,1,0:T(8,128)(2,1)S(1)}, u32[]{:S(2)}, u32[]{:S(2)}) collective-permute-start(bf16[1,2,32,640]{3,2,1,0:T(8,128)(2,1)S(1)} %get-tuple-element.8), channel_id=1, source_target_pairs={{0,112},{8,120},{16,96},{24,104},{32,80},{40,88},{48,64},{56,72},{... | collective-permute-start | bytes 245768 | tf_op jit(solution)/shard_map/ppermute | solution.py:21
  68.0 7.8 %collective-permute-start.14 = (bf16[1,2,32,640]{3,2,1,0:T(8,128)(2,1)S(1)}, bf16[1,2,32,640]{3,2,1,0:T(8,128)(2,1)S(1)}, u32[]{:S(2)}, u32[]{:S(2)}) collective-permute-start(bf16[1,2,32,640]{3,2,1,0:T(8,128)(2,1)S(1)} %get-tuple-element.7), channel_id=1, source_target_pairs={{0,120},{8,112},{16,104},{24,96},{32,88},{40,80},{48,72},{56,64},{... | collective-permute-start | bytes 245768 | tf_op jit(solution)/shard_map/ppermute | solution.py:21
  76.5 1.6 %copy-start.4 = (bf16[8,625,64]{1,2,0:T(8,128)(2,1)S(1)}, bf16[8,625,64]{1,2,0:T(8,128)(2,1)}, u32[]{:S(2)}) copy-start(bf16[8,625,64]{1,2,0:T(8,128)(2,1)} %convolution_convert_fusion) | copy-start | bytes 1920004
  76.7 9.8 %copy-start.1 = (bf16[8,625,625]{2,1,0:T(8,128)(2,1)S(1)}, bf16[8,625,625]{2,1,0:T(8,128)(2,1)}, u32[]{:S(2)}) copy-start(bf16[8,625,625]{2,1,0:T(8,128)(2,1)} %copy.60) | copy-start | bytes 18750004
  78.4 1.2 %collective-permute-start.15 = (f32[32,64]{1,0:T(8,128)S(1)}, f32[32,64]{1,0:T(8,128)S(1)}, u32[]{:S(2)}, u32[]{:S(2)}) collective-permute-start(f32[32,64]{1,0:T(8,128)S(1)} %convolution_bitcast_fusion.1), channel_id=1, source_target_pairs={{0,1},{1,0},{2,3},{3,2},{4,5},{5,4},{6,7},{7,6},{8,9},{9,8},{10,11... | collective-permute-start | bytes 24584 | tf_op jit(solution)/shard_map/ppermute | solution.py:33
  79.6 4.0 %collective-permute-start.16 = (f32[32,64]{1,0:T(8,128)S(1)}, f32[32,64]{1,0:T(8,128)S(1)}, u32[]{:S(2)}, u32[]{:S(2)}) collective-permute-start(f32[32,64]{1,0:T(8,128)S(1)} %add.117), channel_id=1, source_target_pairs={{0,2},{1,3},{2,0},{3,1},{4,6},{5,7},{6,4},{7,5},{8,10},{9,11},{10,... | collective-permute-start | bytes 24584 | tf_op jit(solution)/shard_map/ppermute | solution.py:33
  83.7 5.3 %collective-permute-start.17 = (f32[32,64]{1,0:T(8,128)S(1)}, f32[32,64]{1,0:T(8,128)S(1)}, u32[]{:S(2)}, u32[]{:S(2)}) collective-permute-start(f32[32,64]{1,0:T(8,128)S(1)} %add.118), channel_id=1, source_target_pairs={{0,4},{1,5},{2,6},{3,7},{4,0},{5,1},{6,2},{7,3},{8,12},{9,13},{10,... | collective-permute-start | bytes 24584 | tf_op jit(solution)/shard_map/ppermute | solution.py:33
  86.5 2.5 %copy-start.6 = (f32[1,64,64]{2,1,0:T(8,128)S(1)}, f32[1,64,64]{2,1,0:T(8,128)}, u32[]{:S(2)}) copy-start(f32[1,64,64]{2,1,0:T(8,128)} %param.15) | copy-start | bytes 49156
